TPU v7x, 32 devices: a whole 2x2x4 slice. The times are simulated.
32 devices in a mesh: seq: 4 (over y, x), exp: 8 (over z, core).
Axes of the slice: x: 2, y: 2, z: 4, core: 2. Of those that a mesh axis runs over, the one named last changes fastest.
Arguments:
- token_ids: int32 [4, 32], replicated, may hold values from 0 to 51199
- cache_lengths: int32 [32], replicated, may hold values from 1 to 1024, as said below
- empty_blocks: int32 [32, 64], replicated, may hold values 0 or 1
- expert_ids: int32 [4, 32, 6], replicated, may hold values from 0 to 63, all different within a row
- embed_table: bfloat16 [51200, 2048], P(('seq', 'exp')), may hold values from -3 to 3
- attn_gain: float32 [2048], replicated, may hold values from 0.5 to 1.5
- w_query: bfloat16 [2048, 2048], P(None, 'seq'), may hold values from -0.125 to 0.125
- w_key: bfloat16 [2048, 2048], P(None, 'seq'), may hold values from -0.125 to 0.125
- w_value: bfloat16 [2048, 2048], P(None, 'seq'), may hold values from -0.125 to 0.125
- w_out: bfloat16 [2048, 2048], P('seq'), may hold values from -0.125 to 0.125
- k_cache: bfloat16 [32, 1024, 2048], P('exp', 'seq'), may hold values from -200 to 200
- v_cache: bfloat16 [32, 1024, 2048], P('exp', 'seq'), may hold values from -6 to 6
- moe_gain: float32 [2048], replicated, may hold values from 0.5 to 1.5
- w_router: bfloat16 [2048, 64], replicated, may hold values from -0.125 to 0.125
- gate_pieces: bfloat16 [256, 2048, 352], P(('seq', 'exp')), may hold values from -0.125 to 0.125
- up_pieces: bfloat16 [256, 2048, 352], P(('seq', 'exp')), may hold values from -0.125 to 0.125
- down_pieces: bfloat16 [256, 352, 2048], P(('seq', 'exp')), may hold values from -0.15625 to 0.15625
- shared_gate: bfloat16 [2048, 2816], P(None, 'exp'), may hold values from -0.125 to 0.125
- shared_up: bfloat16 [2048, 2816], P(None, 'exp'), may hold values from -0.125 to 0.125
- shared_down: bfloat16 [2816, 2048], P('exp'), may hold values from -0.109375 to 0.109375
- final_gain: float32 [2048], replicated, may hold values from 0.5 to 1.5
- w_head: bfloat16 [2048, 51200], P(None, ('seq', 'exp')), may hold values from -0.125 to 0.125
Outputs:
- hidden_norms: float32 [4, 32], replicated
- greatest_logits: float32 [4, 32], replicated
Inputs may be any that keep to these rules, and one draw needn't show every extreme that they name: `cache_lengths`: one of the 32 requests has exactly 1024 cached positions in every draw.
All inputs are finite; a program needn't handle non-finite values.
Results may differ from a plain program's by a relative error of at most 0.0055.
Values may be sent and summed in bfloat16 or wider, within the bound.
No kernel may reach another device: no remote copies, remote signals or barrier semaphores. Data moves between devices by JAX's collectives and lax.ppermute only.
A program may use at most 128 MiB of HBM per device.

v0:
```python
import math
import jax
import jax.numpy as jnp
from jax import lax
from jax.sharding import PartitionSpec as P

HDIM = 128
PIECES = 4
BLK = 16
epsilon = 1e-06
negative = -1e30


def rms_scale(values, scales):
    return values * lax.rsqrt(jnp.mean(values * values, axis=-1, keepdims=True) + epsilon) * scales


def rotate(values, places):
    half_width = values.shape[-1] // 2
    frequency = 10000.0 ** (-2.0 * jnp.arange(half_width, dtype=jnp.float32) / values.shape[-1])
    angles = places.astype(jnp.float32)[..., None, None] * frequency
    cosine_table = jnp.cos(angles)
    sine_table = jnp.sin(angles)
    lower = values[..., :half_width]
    upper = values[..., half_width:]
    return jnp.concatenate(
        [lower * cosine_table - upper * sine_table, upper * cosine_table + lower * sine_table],
        axis=-1,
    )


def gather_all(values):
    inner = lax.all_gather(values, "exp", axis=0, tiled=False)
    return lax.all_gather(inner, "seq", axis=0, tiled=False)


def on_device(
    token_ids,
    cache_lengths,
    empty_blocks,
    expert_ids,
    embed_table,
    attn_gain,
    w_query,
    w_key,
    w_value,
    w_out,
    k_cache,
    v_cache,
    moe_gain,
    w_router,
    gate_pieces,
    up_pieces,
    down_pieces,
    shared_gate,
    shared_up,
    shared_down,
    final_gain,
    w_head,
):
    steps, requests = token_ids.shape
    tokens = steps * requests
    width = embed_table.shape[1]
    vocab_local = embed_table.shape[0]
    n_seq = lax.axis_size("seq")
    n_exp = lax.axis_size("exp")
    n_dev = n_seq * n_exp
    owner_index = lax.axis_index(("seq", "exp"))
    seq_index = lax.axis_index("seq")
    own_count = requests // n_exp
    own_start = lax.axis_index("exp") * own_count
    group = steps * own_count
    share = group // n_seq

    def grouped(values):
        rest = values.shape[2:]
        by_group = jnp.moveaxis(values.reshape((steps, n_exp, own_count) + rest), 1, 0)
        return by_group.reshape((tokens,) + rest)

    def natural(values):
        split = jnp.swapaxes(values.reshape(n_seq, n_exp, share), 0, 1)
        grouped = split.reshape(n_exp, steps, own_count)
        return jnp.moveaxis(grouped, 0, 1).reshape(steps, requests)

    group_ids = jnp.moveaxis(token_ids.reshape(steps, n_exp, own_count), 1, 0)
    local_ids = group_ids - owner_index * vocab_local
    held = (local_ids >= 0) & (local_ids < vocab_local)
    rows = jnp.take(embed_table, jnp.clip(local_ids, 0, vocab_local - 1), axis=0)
    rows = jnp.where(held[..., None], rows, jnp.zeros((), rows.dtype))
    arrived = lax.all_to_all(rows, "exp", 0, 0, tiled=True)
    row_part = jnp.sum(arrived.astype(jnp.float32), axis=0).astype(jnp.bfloat16)
    row_parts = lax.all_gather(row_part, "seq", axis=0, tiled=False)
    embedded = jnp.sum(row_parts.astype(jnp.float32), axis=0).reshape(group, width)
    attn_in = rms_scale(embedded, attn_gain).astype(jnp.bfloat16)
    own_lengths = lax.dynamic_slice_in_dim(cache_lengths, own_start, own_count, 0)
    places = (own_lengths[None, :] + jnp.arange(steps, dtype=jnp.int32)[:, None]).reshape(group)
    heads_here = w_query.shape[1] // HDIM

    def project(weight):
        return jnp.dot(attn_in, weight, preferred_element_type=jnp.float32).reshape(
            group, heads_here, HDIM
        )

    query_part = rotate(project(w_query), places).astype(jnp.bfloat16)
    key_part = rotate(project(w_key), places).astype(jnp.bfloat16)
    value_part = project(w_value).astype(jnp.bfloat16)
    every = lax.all_gather(
        jnp.stack([query_part, key_part, value_part], axis=0), "seq", axis=0, tiled=False
    )
    head_count = n_seq * heads_here
    every = jnp.moveaxis(every, 0, 2).reshape(3, steps, own_count, head_count, HDIM)
    queries = every[0]
    span = k_cache.shape[1]
    first_place = seq_index * span
    places_here = first_place + jnp.arange(span, dtype=jnp.int32)
    own_empty = lax.dynamic_slice_in_dim(empty_blocks, own_start, own_count, 0)
    local_blocks = lax.dynamic_slice_in_dim(own_empty, first_place // BLK, span // BLK, 1)
    blocked = jnp.broadcast_to(local_blocks[:, :, None], (own_count, span // BLK, BLK)).reshape(
        own_count, span
    )
    live_mask = ((places_here[None, :] < own_lengths[:, None]) & (blocked == 0))[None, :, None, :]
    cache_keys = k_cache.reshape(own_count, span, head_count, HDIM)
    cache_values = v_cache.reshape(own_count, span, head_count, HDIM)
    score_scale = 1.0 / math.sqrt(HDIM)
    cached = (
        jnp.einsum("trhd,rphd->trhp", queries, cache_keys, preferred_element_type=jnp.float32)
        * score_scale
    )
    local_top = jnp.max(jnp.where(live_mask, cached, negative), axis=3)
    local_weights = jnp.where(live_mask, jnp.exp(cached - local_top[..., None]), 0.0)
    local_totals = jnp.sum(local_weights, axis=3)
    local_mixture = jnp.einsum(
        "trhp,rphd->trhd",
        local_weights.astype(jnp.bfloat16),
        cache_values,
        preferred_element_type=jnp.float32,
    )

    def by_owner(values):
        rest = values.shape[3:]
        split = values.reshape((steps, own_count, n_seq, heads_here) + rest)
        return jnp.moveaxis(split, 2, 0).reshape(n_seq, -1)

    mix_len = group * heads_here * HDIM
    stat_len = group * heads_here
    packed = jnp.concatenate(
        [by_owner(local_mixture), by_owner(local_top), by_owner(local_totals)], axis=1
    )
    got = lax.all_to_all(packed, "seq", 0, 0, tiled=True)
    got_mixture = got[:, :mix_len].reshape(n_seq, steps, own_count, heads_here, HDIM)
    got_top = got[:, mix_len : mix_len + stat_len].reshape(n_seq, steps, own_count, heads_here)
    got_totals = got[:, mix_len + stat_len :].reshape(n_seq, steps, own_count, heads_here)
    own_queries = query_part.reshape(steps, own_count, heads_here, HDIM)
    own_keys = key_part.reshape(steps, own_count, heads_here, HDIM)
    own_values = value_part.reshape(steps, own_count, heads_here, HDIM)
    fresh_scores = (
        jnp.einsum("trhd,urhd->trhu", own_queries, own_keys, preferred_element_type=jnp.float32)
        * score_scale
    )
    causal = (jnp.arange(steps)[None, :] <= jnp.arange(steps)[:, None])[:, None, None, :]
    fresh_top = jnp.max(jnp.where(causal, fresh_scores, negative), axis=3)
    fresh_weights = jnp.where(causal, jnp.exp(fresh_scores - fresh_top[..., None]), 0.0)
    fresh_mixture = jnp.einsum(
        "trhu,urhd->trhd",
        fresh_weights.astype(jnp.bfloat16),
        own_values,
        preferred_element_type=jnp.float32,
    )
    top_score = jnp.maximum(jnp.max(got_top, axis=0), fresh_top)
    cache_factor = jnp.exp(got_top - top_score[None])
    fresh_factor = jnp.exp(fresh_top - top_score)
    totals = (
        jnp.sum(got_totals * cache_factor, axis=0) + jnp.sum(fresh_weights, axis=3) * fresh_factor
    )
    mixture = (
        jnp.sum(got_mixture * cache_factor[..., None], axis=0)
        + fresh_mixture * fresh_factor[..., None]
    )
    own_heads = (mixture / totals[..., None]).astype(jnp.bfloat16).reshape(group, heads_here * HDIM)
    attn_part = jnp.dot(own_heads, w_out, preferred_element_type=jnp.float32)
    resid_group = embedded + jnp.sum(lax.all_gather(attn_part, "seq", axis=0, tiled=False), axis=0)
    resid_share = lax.dynamic_slice_in_dim(resid_group, seq_index * share, share, 0)
    moe_in = lax.all_gather(
        rms_scale(resid_group, moe_gain).astype(jnp.bfloat16), "exp", axis=0, tiled=True
    )
    router = jax.nn.sigmoid(jnp.dot(moe_in, w_router, preferred_element_type=jnp.float32))
    expert_count = w_router.shape[1]
    chosen_ids = grouped(expert_ids)
    picked = chosen_ids[:, :, None] == jnp.arange(expert_count, dtype=jnp.int32)[None, None, :]
    chosen = jnp.sum(jnp.where(picked, router[:, None, :], 0.0), axis=2)
    gate_weights = chosen / jnp.sum(chosen, axis=1, keepdims=True)
    rows_here = gate_pieces.shape[0]
    row_expert = (owner_index * rows_here + jnp.arange(rows_here, dtype=jnp.int32)) // PIECES
    token_weight = jnp.sum(
        jnp.where(
            chosen_ids[None, :, :] == row_expert[:, None, None], gate_weights[None, :, :], 0.0
        ),
        axis=2,
    )
    gate_out = jnp.einsum("nd,jdf->jnf", moe_in, gate_pieces, preferred_element_type=jnp.float32)
    up_out = jnp.einsum("nd,jdf->jnf", moe_in, up_pieces, preferred_element_type=jnp.float32)
    weighted_hidden = (jax.nn.silu(gate_out) * up_out * token_weight[:, :, None]).astype(
        jnp.bfloat16
    )
    routed = jnp.einsum(
        "jnf,jfd->nd", weighted_hidden, down_pieces, preferred_element_type=jnp.float32
    )
    share_count = tokens // n_seq
    share_start = seq_index * share_count
    share_rows = lax.dynamic_slice_in_dim(moe_in, share_start, share_count, 0)
    shared_hidden = (
        jax.nn.silu(jnp.dot(share_rows, shared_gate, preferred_element_type=jnp.float32))
        * jnp.dot(share_rows, shared_up, preferred_element_type=jnp.float32)
    ).astype(jnp.bfloat16)
    shared_out = jnp.dot(shared_hidden, shared_down, preferred_element_type=jnp.float32)
    term_rows = lax.dynamic_update_slice_in_dim(
        routed,
        lax.dynamic_slice_in_dim(routed, share_start, share_count, 0) + shared_out,
        share_start,
        0,
    )
    term_rows = jnp.swapaxes(term_rows.reshape(n_exp, n_seq, share, width), 0, 1)
    term_sum = jnp.sum(
        lax.all_to_all(
            term_rows.reshape(n_dev, share, width).astype(jnp.bfloat16),
            ("seq", "exp"),
            0,
            0,
            tiled=True,
        ).astype(jnp.float32),
        axis=0,
    )
    final_share = resid_share + term_sum
    norms_share = jnp.sqrt(jnp.mean(final_share * final_share, axis=-1))
    head_in = gather_all(rms_scale(final_share, final_gain).astype(jnp.bfloat16)).reshape(
        tokens, width
    )
    local_best = jnp.max(jnp.dot(head_in, w_head, preferred_element_type=jnp.float32), axis=-1)
    message = jnp.concatenate([local_best, norms_share], axis=0)
    heard = lax.all_to_all(
        jnp.broadcast_to(message[None, :], (n_dev, message.shape[0])),
        ("seq", "exp"),
        0,
        0,
        tiled=True,
    )
    greatest_logits = natural(jnp.max(heard[:, :tokens], axis=0))
    hidden_norms = natural(heard[:, tokens:].reshape(tokens))
    return (hidden_norms, greatest_logits)


def solution(mesh):
    in_specs = (
        P(),
        P(),
        P(),
        P(),
        P(("seq", "exp"), None),
        P(),
        P(None, "seq"),
        P(None, "seq"),
        P(None, "seq"),
        P("seq", None),
        P("exp", "seq", None),
        P("exp", "seq", None),
        P(),
        P(),
        P(("seq", "exp"), None, None),
        P(("seq", "exp"), None, None),
        P(("seq", "exp"), None, None),
        P(None, "exp"),
        P(None, "exp"),
        P("exp", None),
        P(),
        P(None, ("seq", "exp")),
    )
    out_specs = (P(), P())
    return jax.shard_map(
        on_device, mesh=mesh, in_specs=in_specs, out_specs=out_specs, check_vma=False
    )
```

profile of v0, /device:TPU:0, one launch (start us, length us, event | category | flops | bytes accessed | tf_op | source)
XLA Modules:
  0.0 184.5 jit_solution(12790132844402433581)
XLA Ops:
  2.4 5.1 %gather_fusion = bf16[128,2048]{1,0:T(8,128)(2,1)S(1)} fusion(bf16[1600,2048]{1,0:T(8,128)(2,1)} %param.26, s32[1024]{0:T(1024)S(1)} %pad_clamp_fusion), kind=kCustom, calls=%fused_computation | custom fusion | bytes 1049088 | tf_op jit(solution)/shard_map/jit(_take)/gather | solution.py:88
  9.1 6.3 %all-to-all-start = ((bf16[8,4,4,2048]{3,2,1,0:T(4,128)(2,1)}), bf16[8,4,4,2048]{3,2,1,0:T(4,128)(2,1)S(1)}, u32[]{:S(2)}, u32[]{:S(2)}) async-start(bf16[8,4,4,2048]{3,2,1,0:T(4,128)(2,1)} %select_select_fusion), calls=%async_computation | async-start | bytes 1048576 | tf_op jit(solution)/shard_map/all_to_all | solution.py:90
  16.3 4.0 %copy.166 = bf16[512,2048]{1,0:T(8,128)(2,1)} copy(bf16[512,2048]{0,1:T(8,128)(2,1)} %bitcast.153) | data formatting | bytes 4194304 | tf_op jit(solution)/shard_map/dot_general | solution.py:100
  20.3 3.9 %copy.167 = bf16[512,2048]{1,0:T(8,128)(2,1)} copy(bf16[512,2048]{0,1:T(8,128)(2,1)} %bitcast.154) | data formatting | bytes 4194304 | tf_op jit(solution)/shard_map/dot_general | solution.py:100
  24.3 4.0 %copy.168 = bf16[512,2048]{1,0:T(8,128)(2,1)} copy(bf16[512,2048]{0,1:T(8,128)(2,1)} %bitcast.155) | data formatting | bytes 4194304 | tf_op jit(solution)/shard_map/dot_general | solution.py:100
  31.1 9.0 %all-gather = bf16[16,4,2048]{2,1,0:T(4,128)(2,1)S(1)} all-gather(bf16[4,4,2048]{2,1,0:T(4,128)(2,1)S(1)} %reduce_sum.137), channel_id=2, replica_groups=mesh['seq'=4,'exp'=8] {'seq'}, dimensions={0}, use_global_device_ids=true | all-gather | bytes 327680 | tf_op jit(solution)/shard_map/all_gather | solution.py:92
  40.5 2.4 %fusion.72 = f32[16,4,128]{2,0,1:T(8,128)S(1)} fusion(bf16[16,2048,1]{1,0,2:T(8,128)(2,1)S(1)} %reshape.577, bf16[4,128,2048]{2,1,0:T(8,128)(2,1)} %bitcast.151), kind=kOutput, calls=%fused_computation.132 | convolution fusion | flops 33554432 | bytes 2195456 | tf_op jit(solution)/shard_map/dot_general | solution.py:100
  44.2 2.2 %convolution_convert_fusion = bf16[16,4,128]{2,0,1:T(8,128)(2,1)S(1)} fusion(bf16[16,2048,1]{1,0,2:T(8,128)(2,1)S(1)} %reshape.577, bf16[4,128,2048]{2,1,0:T(8,128)(2,1)} %bitcast.149), kind=kOutput, calls=%fused_computation.31 | convolution fusion | flops 33562624 | bytes 2179072 | tf_op jit(solution)/shard_map/dot_general | solution.py:100
  46.6 8.8 %all-gather.1 = bf16[12,16,4,128]{3,1,2,0:T(8,128)(2,1)S(1)} all-gather(bf16[3,16,4,128]{3,1,2,0:T(8,128)(2,1)S(1)} %pad_maximum_fusion), channel_id=3, replica_groups=mesh['seq'=4,'exp'=8] {'seq'}, dimensions={0}, use_global_device_ids=true | all-gather | bytes 245760 | tf_op jit(solution)/shard_map/all_gather | solution.py:107
  55.5 3.5 %select_reduce_fusion = (f32[4,4,16]{0,2,1:T(8,128)S(1)}, f32[4,4,16,256]{3,0,2,1:T(4,128)S(1)}) fusion(pred[4,256]{1,0:T(4,128)(4,1)S(1)} %compare_and_fusion.1, bf16[4,4,16,128]{3,2,1,0:T(8,128)(2,1)S(1)} %bitcast.185, bf16[4,256,2048]{2,1,0:T(8,128)(2,1)} %param.32), kind=kOutput, calls=%fused_computation.39 | convolution fusion | flops 16973568 | bytes 4524032 | tf_op jit(solution)/shard_map/trhd,rphd->trhp/dot_general | solution.py:126
  59.6 2.9 %fusion = f32[4,16,4,128]{3,2,1,0:T(4,128)S(1)} fusion(f32[4,4,16,256]{3,0,2,1:T(4,128)S(1)} %get-tuple-element.22, f32[4,4,16]{0,2,1:T(8,128)S(1)} %get-tuple-element.21, pred[4,256]{1,0:T(4,128)(4,1)S(1)} %compare_and_fusion.1, bf16[4,256,2048]{2,1,0:T(8,128)(2,1)} %param.33), kind=kOutput, calls=%fused_computation.1 | convolution fusion | flops 16973824 | bytes 4589568 | tf_op jit(solution)/shard_map/trhp,rphd->trhd/dot_general | solution.py:132
  63.8 3.3 %all-to-all-start.1 = ((f32[4,1,8320]{2,1,0:T(1,128)}), f32[4,1,8320]{2,1,0:T(1,128)S(1)}, u32[]{:S(2)}, u32[]{:S(2)}) async-start(f32[4,1,8320]{2,1,0:T(1,128)} %copy.149), calls=%async_computation.1 | async-start | bytes 266240 | tf_op jit(solution)/shard_map/all_to_all | solution.py:149
  67.2 4.9 %all-to-all-done.1 = f32[4,1,8320]{2,1,0:T(1,128)S(1)} async-done(((f32[4,1,8320]{2,1,0:T(1,128)}), f32[4,1,8320]{2,1,0:T(1,128)S(1)}, u32[]{:S(2)}, u32[]{:S(2)}) %all-to-all-start.1) | async-done | bytes 133152 | tf_op jit(solution)/shard_map/all_to_all | solution.py:149
  74.0 9.4 %all-gather.2 = f32[64,2048]{1,0:T(8,128)S(1)} all-gather(f32[16,2048]{1,0:T(8,128)S(1)} %fusion.50), channel_id=4, replica_groups=mesh['seq'=4,'exp'=8] {'seq'}, dimensions={0}, use_global_device_ids=true | all-gather | bytes 655360 | tf_op jit(solution)/shard_map/all_gather | solution.py:181
  83.7 15.0 %all_gather.39 = bf16[128,2048]{1,0:T(8,128)(2,1)S(1)} all-gather(bf16[16,2048]{1,0:T(8,128)(2,1)S(1)} %multiply_convert_fusion), channel_id=1, replica_groups=mesh['seq'=4,'exp'=8] {'exp'}, dimensions={0}, use_global_device_ids=true | all-gather | bytes 589824 | tf_op jit(solution)/shard_map/all_gather | solution.py:183
  99.0 6.1 %convolution_bitcast_fusion.2 = f32[8,128,352]{1,2,0:T(8,128)S(1)} fusion(bf16[8,2048,352]{1,2,0:T(8,128)(2,1)} %param.36, bf16[128,2048]{1,0:T(8,128)(2,1)S(1)} %all_gather.39), kind=kOutput, calls=%fused_computation.11 | convolution fusion | flops 1476395008 | bytes 13500416 | tf_op jit(solution)/shard_map/nd,jdf->jnf/dot_general | solution.py:200
  105.9 14.7 %convolution_bitcast_fusion = f32[128,2048]{1,0:T(8,128)S(1)} fusion(bf16[8,352,2048]{2,1,0:T(8,128)(2,1)} %param.38, bf16[8,2048,352]{1,2,0:T(8,128)(2,1)} %param.37, f32[8,128,352]{1,2,0:T(8,128)S(1)} %convolution_bitcast_fusion.2, f32[8,128]{1,0:T(8,128)S(1)} %select_reduce_fusion.4, bf16[128,2048]{1,0:T(8,128)(2,1)S(1)} %all_gather.39), kind=kOutput, calls=%fused_computation.7 | convolution fusion | flops 2955313152 | bytes 26087424 | tf_op jit(solution)/shard_map/jnf,jfd->nd/dot_general | solution.py:205
  120.6 2.9 %fusion.6 = f32[128,2048]{1,0:T(8,128)S(1)} fusion(f32[128,2048]{1,0:T(8,128)S(1)} %convolution_bitcast_fusion, s32[]{:T(128)S(6)} %select_n.84, bf16[352,2048]{1,0:T(8,128)(2,1)} %param.41, bf16[2048,352]{0,1:T(8,128)(2,1)} %param.40, bf16[128,2048]{1,0:T(8,128)(2,1)S(1)} %all_gather.39, f32[32,352]{1,0:T(8,128)S(1)} %fusion.37), kind=kOutput, calls=%fused_computation.9 | convolution fusion | flops 92407808 | bytes 3589120 | tf_op jit(solution)/shard_map/dot_general | solution.py:215
  125.3 3.3 %all-to-all-start.2 = ((bf16[32,4,2048]{2,1,0:T(4,128)(2,1)}), bf16[32,4,2048]{2,1,0:T(4,128)(2,1)S(1)}, u32[]{:S(2)}, u32[]{:S(2)}) async-start(bf16[32,4,2048]{2,1,0:T(4,128)(2,1)} %copy.164), calls=%async_computation.2 | async-start | bytes 1048576 | tf_op jit(solution)/shard_map/all_to_all | solution.py:224
  128.6 16.4 %all-to-all-done.2 = bf16[32,4,2048]{2,1,0:T(4,128)(2,1)S(1)} async-done(((bf16[32,4,2048]{2,1,0:T(4,128)(2,1)}), bf16[32,4,2048]{2,1,0:T(4,128)(2,1)S(1)}, u32[]{:S(2)}, u32[]{:S(2)}) %all-to-all-start.2) | async-done | bytes 524320 | tf_op jit(solution)/shard_map/all_to_all | solution.py:224
  145.4 14.0 %all-gather.5 = bf16[8,4,2048]{2,1,0:T(4,128)(2,1)S(1)} all-gather(bf16[1,4,2048]{2,1,0:T(4,128)(2,1)S(1)} %fusion.49), channel_id=5, replica_groups=mesh['seq'=4,'exp'=8] {'exp'}, dimensions={0}, use_global_device_ids=true | all-gather | bytes 147456 | tf_op jit(solution)/shard_map/all_gather | solution.py:33
  159.3 9.4 %all-gather.4 = bf16[32,4,2048]{2,1,0:T(4,128)(2,1)S(1)} all-gather(bf16[8,4,2048]{2,1,0:T(4,128)(2,1)S(1)} %all-gather.5), channel_id=6, replica_groups=mesh['seq'=4,'exp'=8] {'seq'}, dimensions={0}, use_global_device_ids=true | all-gather | bytes 655360 | tf_op jit(solution)/shard_map/all_gather | solution.py:34
  168.9 4.9 %convolution_reduce_fusion = f32[128]{0:T(128)S(1)} fusion(bf16[128,2048]{1,0:T(8,128)(2,1)S(1)} %reshape.556, bf16[2048,1600]{0,1:T(8,128)(2,1)} %param.43), kind=kOutput, calls=%fused_computation.15 | convolution fusion | flops 839065472 | bytes 7078400 | tf_op jit(solution)/shard_map/dot_general | solution.py:238
  173.8 9.3 %all_to_all.31 = f32[32,1,132]{2,1,0:T(1,128)S(1)} all-to-all(f32[32,1,132]{2,1,0:T(1,128)S(1)} %broadcast_in_dim.145), channel_id=1, replica_groups=mesh['seq'=4,'exp'=8] {'seq','exp'}, dimensions={0} | all-to-all | bytes 33792 | tf_op jit(solution)/shard_map/all_to_all | solution.py:240
  (121 shorter events, 17.5 us)
Async XLA Ops:
  0.6 72.9 %copy-start = (bf16[512,2048]{1,0:T(8,128)(2,1)S(1)}, bf16[512,2048]{1,0:T(8,128)(2,1)}, u32[]{:S(2)}) copy-start(bf16[512,2048]{1,0:T(8,128)(2,1)} %param.31) | copy-start | bytes 6291460
  7.6 7.9 %copy-start.9 = (s32[32]{0:T(128)S(1)}, s32[32]{0:T(128)}, u32[]{:S(2)}) copy-start(s32[32]{0:T(128)} %param.23) | copy-start | bytes 388
  9.1 21.7 %all-to-all-start = ((bf16[8,4,4,2048]{3,2,1,0:T(4,128)(2,1)}), bf16[8,4,4,2048]{3,2,1,0:T(4,128)(2,1)S(1)}, u32[]{:S(2)}, u32[]{:S(2)}) async-start(bf16[8,4,4,2048]{3,2,1,0:T(4,128)(2,1)} %select_select_fusion), calls=%async_computation | async-start | bytes 1048576 | tf_op jit(solution)/shard_map/all_to_all | solution.py:90
  24.3 4.2 %copy-start.5 = (s32[4,32,6]{1,0,2:T(4,128)S(1)}, s32[4,32,6]{1,0,2:T(4,128)}, u32[]{:S(2)}) copy-start(s32[4,32,6]{1,0,2:T(4,128)} %param.25) | copy-start | bytes 9220
  28.3 12.1 %copy-start.6 = (f32[2048]{0:T(1024)S(1)}, f32[2048]{0:T(1024)}, u32[]{:S(2)}) copy-start(f32[2048]{0:T(1024)} %param.27) | copy-start | bytes 24580
  40.5 2.4 %copy-start.2 = (bf16[512,2048]{1,0:T(8,128)(2,1)S(1)}, bf16[512,2048]{1,0:T(8,128)(2,1)}, u32[]{:S(2)}) copy-start(bf16[512,2048]{1,0:T(8,128)(2,1)} %copy.167) | copy-start | bytes 6291460
  63.8 8.3 %all-to-all-start.1 = ((f32[4,1,8320]{2,1,0:T(1,128)}), f32[4,1,8320]{2,1,0:T(1,128)S(1)}, u32[]{:S(2)}, u32[]{:S(2)}) async-start(f32[4,1,8320]{2,1,0:T(1,128)} %copy.149), calls=%async_computation.1 | async-start | bytes 266240 | tf_op jit(solution)/shard_map/all_to_all | solution.py:149
  73.5 10.1 %copy-start.7 = (f32[2048]{0:T(1024)S(1)}, f32[2048]{0:T(1024)}, u32[]{:S(2)}) copy-start(f32[2048]{0:T(1024)} %param.34) | copy-start | bytes 24580
  73.6 25.2 %copy-start.4 = (bf16[2048,64]{0,1:T(8,128)(2,1)S(1)}, bf16[2048,64]{0,1:T(8,128)(2,1)}, u32[]{:S(2)}) copy-start(bf16[2048,64]{0,1:T(8,128)(2,1)} %param.35) | copy-start | bytes 786436
  99.0 6.3 %copy-start.3 = (bf16[2048,352]{0,1:T(8,128)(2,1)S(1)}, bf16[2048,352]{0,1:T(8,128)(2,1)}, u32[]{:S(2)}) copy-start(bf16[2048,352]{0,1:T(8,128)(2,1)} %param.39) | copy-start | bytes 4325380
  123.8 21.5 %copy-start.8 = (f32[2048]{0:T(1024)S(1)}, f32[2048]{0:T(1024)}, u32[]{:S(2)}) copy-start(f32[2048]{0:T(1024)} %param.42) | copy-start | bytes 24580
  125.3 19.6 %all-to-all-start.2 = ((bf16[32,4,2048]{2,1,0:T(4,128)(2,1)}), bf16[32,4,2048]{2,1,0:T(4,128)(2,1)S(1)}, u32[]{:S(2)}, u32[]{:S(2)}) async-start(bf16[32,4,2048]{2,1,0:T(4,128)(2,1)} %copy.164), calls=%async_computation.2 | async-start | bytes 1048576 | tf_op jit(solution)/shard_map/all_to_all | solution.py:224
  168.8 15.6 %copy-start.1 = (bf16[512,2048]{1,0:T(8,128)(2,1)S(1)}, bf16[512,2048]{1,0:T(8,128)(2,1)}, u32[]{:S(2)}) copy-start(bf16[512,2048]{1,0:T(8,128)(2,1)} %param.31) | copy-start | bytes 6291460
where the time goes:
time: 185 us; the launch traced here: 184 us
  blocking collectives  75 us (41%)
  matrix products  42 us (23%)
  local copies, waits for them, and re-layouts  24.2 us (13%)
  waiting for transfers between devices  23.1 us (12%)
  starting transfers between devices  12.9 us (7%)
  other arithmetic  6.12 us (3%)
    all_to_all x1, waiting for transfers between devices, on_device(): lax.all_to_all(term_rows.reshape(n_dev, share, width).astype(jnp.bfloat16...  16.4 us
    all_gather x1, blocking collectives, on_device(): lax.all_gather(rms_scale(resid_group, moe_gain).astype(jnp.bfloat16), 'ex...  15 us
    dot_general x1, matrix products, on_device(): jnp.einsum('jnf,jfd->nd', weighted_hidden, down_pieces, preferred_element...  14.7 us
    all_gather x1, blocking collectives, gather_all(): inner = lax.all_gather(values, 'exp', axis=0, tiled=False)  14 us
    dot_general x3, local copies, waits for them, and re-layouts, project(): jnp.dot(attn_in, weight, preferred_element_type=jnp.float32)  11.9 us
    all_gather x1, blocking collectives, on_device(): lax.all_gather(attn_part, 'seq', axis=0, tiled=False)  9.45 us
    all_gather x1, blocking collectives, gather_all(): return lax.all_gather(inner, 'seq', axis=0, tiled=False)  9.37 us
    all_to_all x1, blocking collectives, on_device(): lax.all_to_all(jnp.broadcast_to(message[None, :], (n_dev, message.shape[0...  9.32 us
  transfers between devices with their start and end apart: 3, of which 3 were waited for; matrix products, arithmetic and copies ran while one was open for 7% of the time, Pallas kernels for 0%

commit v1 on v0

--- a/solution.py
+++ b/solution.py
@@ -9,6 +9,17 @@
 BLK = 16
 epsilon = 1e-06
 negative = -1e30
+
+
+def cut_along(value, dim, size):
+    before, after = (value.shape[:dim], value.shape[dim + 1 :])
+    return jnp.moveaxis(value.reshape(*before, size, -1, *after), dim, 0)
+
+
+def joined_along(pieces, dim):
+    pieces = jnp.moveaxis(pieces, 0, dim)
+    lengths = pieces.shape
+    return pieces.reshape(*lengths[:dim], lengths[dim] * lengths[dim + 1], *lengths[dim + 2 :])
 
 
 def rms_scale(values, scales):
@@ -146,7 +157,14 @@
     packed = jnp.concatenate(
         [by_owner(local_mixture), by_owner(local_top), by_owner(local_totals)], axis=1
     )
-    got = lax.all_to_all(packed, "seq", 0, 0, tiled=True)
+    devices, index = (lax.axis_size("seq"), lax.axis_index("seq"))
+    tiles = cut_along(packed, 0, devices)
+    outs = [tiles[index]]
+    for step in range(1, devices):
+        sent = tiles[index ^ step]
+        outs.append(lax.ppermute(sent, "seq", [(i, i ^ step) for i in range(devices)]))
+    tiles = jnp.stack(outs)[index ^ jnp.arange(devices)]
+    got = joined_along(tiles, 0)
     got_mixture = got[:, :mix_len].reshape(n_seq, steps, own_count, heads_here, HDIM)
     got_top = got[:, mix_len : mix_len + stat_len].reshape(n_seq, steps, own_count, heads_here)
     got_totals = got[:, mix_len + stat_len :].reshape(n_seq, steps, own_count, heads_here)

time: 185 us -> 182 us (0.984)
  waiting for transfers between devices: 23.1 us -> 20.9 us
    all_to_all x1 -> x0, waiting for transfers between devices: 4.95 us -> none  [on_device(): got = lax.all_to_all(packed, 'seq', 0, 0, tiled=True)]
    ppermute x0 -> x3, starting transfers between devices: none -> 3.55 us  [on_device(): lax.ppermute(sent, 'seq', [(i, i ^ step) for i in range(devices)])]
    all_to_all x1 -> x0, starting transfers between devices: 3.32 us -> none  [on_device(): got = lax.all_to_all(packed, 'seq', 0, 0, tiled=True)]
    ppermute x0 -> x3, waiting for transfers between devices: none -> 2.81 us  [on_device(): lax.ppermute(sent, 'seq', [(i, i ^ step) for i in range(devices)])]
  transfers between devices with their start and end apart: 3 -> 5, of which waited for: 3 -> 4; matrix products, arithmetic and copies ran while one was open for 7% -> 8% of each run, Pallas kernels for 0% -> 0%
where the time goes in v1:
time: 182 us; the launch traced here: 181 us
  blocking collectives  74.6 us (41%)
  matrix products  40.4 us (22%)
  local copies, waits for them, and re-layouts  24.2 us (13%)
  waiting for transfers between devices  20.9 us (11%)
  starting transfers between devices  13.4 us (7%)
  other arithmetic  6.26 us (3%)
    all_to_all x1, waiting for transfers between devices, on_device(): lax.all_to_all(term_rows.reshape(n_dev, share, width).astype(jnp.bfloat16...  16.4 us
    all_gather x1, blocking collectives, on_device(): lax.all_gather(rms_scale(resid_group, moe_gain).astype(jnp.bfloat16), 'ex...  15.1 us
    dot_general x1, matrix products, on_device(): jnp.einsum('jnf,jfd->nd', weighted_hidden, down_pieces, preferred_element...  14.7 us
    all_gather x1, blocking collectives, gather_all(): inner = lax.all_gather(values, 'exp', axis=0, tiled=False)  14 us
    dot_general x3, local copies, waits for them, and re-layouts, project(): jnp.dot(attn_in, weight, preferred_element_type=jnp.float32)  11.9 us
    all_gather x1, blocking collectives, gather_all(): return lax.all_gather(inner, 'seq', axis=0, tiled=False)  9.37 us
    all_to_all x1, blocking collectives, on_device(): lax.all_to_all(jnp.broadcast_to(message[None, :], (n_dev, message.shape[0...  9.33 us
    all_gather x1, blocking collectives, on_device(): row_parts = lax.all_gather(row_part, 'seq', axis=0, tiled=False)  9 us
  transfers between devices with their start and end apart: 5, of which 4 were waited for; matrix products, arithmetic and copies ran while one was open for 8% of the time, Pallas kernels for 0%

profile of v1, /device:TPU:0, one launch (start us, length us, event | category | flops | bytes accessed | tf_op | source)
XLA Modules:
  0.0 180.8 jit_solution(12248574632453905633)
XLA Ops:
  2.4 5.1 %gather_fusion = bf16[128,2048]{1,0:T(8,128)(2,1)S(1)} fusion(bf16[1600,2048]{1,0:T(8,128)(2,1)} %param.26, s32[1024]{0:T(1024)S(1)} %pad_clamp_fusion.1), kind=kCustom, calls=%fused_computation | custom fusion | bytes 1049088 | tf_op jit(solution)/shard_map/jit(_take)/gather | solution.py:99
  9.1 6.3 %all-to-all-start = ((bf16[8,4,4,2048]{3,2,1,0:T(4,128)(2,1)}), bf16[8,4,4,2048]{3,2,1,0:T(4,128)(2,1)S(1)}, u32[]{:S(2)}, u32[]{:S(2)}) async-start(bf16[8,4,4,2048]{3,2,1,0:T(4,128)(2,1)} %select_select_fusion), calls=%async_computation | async-start | bytes 1048576 | tf_op jit(solution)/shard_map/all_to_all | solution.py:101
  16.4 4.0 %copy.164 = bf16[512,2048]{1,0:T(8,128)(2,1)} copy(bf16[512,2048]{0,1:T(8,128)(2,1)} %bitcast.158) | data formatting | bytes 4194304 | tf_op jit(solution)/shard_map/dot_general | solution.py:111
  20.3 3.9 %copy.165 = bf16[512,2048]{1,0:T(8,128)(2,1)} copy(bf16[512,2048]{0,1:T(8,128)(2,1)} %bitcast.159) | data formatting | bytes 4194304 | tf_op jit(solution)/shard_map/dot_general | solution.py:111
  24.3 4.0 %copy.166 = bf16[512,2048]{1,0:T(8,128)(2,1)} copy(bf16[512,2048]{0,1:T(8,128)(2,1)} %bitcast.160) | data formatting | bytes 4194304 | tf_op jit(solution)/shard_map/dot_general | solution.py:111
  29.1 1.7 all-to-all-done
  31.1 9.0 %all-gather = bf16[16,4,2048]{2,1,0:T(4,128)(2,1)S(1)} all-gather(bf16[4,4,2048]{2,1,0:T(4,128)(2,1)S(1)} %reduce_sum.137), channel_id=2, replica_groups=mesh['seq'=4,'exp'=8] {'seq'}, dimensions={0}, use_global_device_ids=true | all-gather | bytes 327680 | tf_op jit(solution)/shard_map/all_gather | solution.py:103
  40.5 2.4 %fusion.73 = f32[16,4,128]{2,0,1:T(8,128)S(1)} fusion(bf16[16,2048,1]{1,0,2:T(8,128)(2,1)S(1)} %reshape.614, bf16[4,128,2048]{2,1,0:T(8,128)(2,1)} %bitcast.156), kind=kOutput, calls=%fused_computation.140 | convolution fusion | flops 33554432 | bytes 2195456 | tf_op jit(solution)/shard_map/dot_general | solution.py:111
  44.5 8.8 %all-gather.1 = bf16[12,16,4,128]{3,1,2,0:T(8,128)(2,1)S(1)} all-gather(bf16[3,16,4,128]{3,1,2,0:T(8,128)(2,1)S(1)} %pad_maximum_fusion), channel_id=3, replica_groups=mesh['seq'=4,'exp'=8] {'seq'}, dimensions={0}, use_global_device_ids=true | all-gather | bytes 245760 | tf_op jit(solution)/shard_map/all_gather | solution.py:118
  53.4 3.5 %select_reduce_fusion = (f32[4,4,16]{0,2,1:T(8,128)S(1)}, f32[4,4,16,256]{3,0,2,1:T(4,128)S(1)}) fusion(pred[4,256]{1,0:T(4,128)(4,1)S(1)} %compare_and_fusion.1, bf16[4,4,16,128]{3,2,1,0:T(8,128)(2,1)S(1)} %bitcast.186, bf16[4,256,2048]{2,1,0:T(8,128)(2,1)} %param.32), kind=kOutput, calls=%fused_computation.40 | convolution fusion | flops 16973568 | bytes 4524032 | tf_op jit(solution)/shard_map/trhd,rphd->trhp/dot_general | solution.py:137
  57.5 2.9 %fusion = f32[4,16,4,128]{3,2,1,0:T(4,128)S(1)} fusion(f32[4,4,16,256]{3,0,2,1:T(4,128)S(1)} %get-tuple-element.26, f32[4,4,16]{0,2,1:T(8,128)S(1)} %get-tuple-element.25, pred[4,256]{1,0:T(4,128)(4,1)S(1)} %compare_and_fusion.1, bf16[4,256,2048]{2,1,0:T(8,128)(2,1)} %param.33), kind=kOutput, calls=%fused_computation.2 | convolution fusion | flops 16973824 | bytes 4589568 | tf_op jit(solution)/shard_map/trhp,rphd->trhd/dot_general | solution.py:143
  61.5 1.6 collective-permute-start.1
  65.5 2.5 %collective-permute-done.2 = f32[1,8320]{1,0:T(1,128)S(1)} collective-permute-done((f32[1,8320]{1,0:T(1,128)S(1)}, f32[1,8320]{1,0:T(1,128)S(1)}, u32[]{:S(2)}, u32[]{:S(2)}) %collective-permute-start.2) | collective-permute-done | bytes 33312 | tf_op jit(solution)/shard_map/ppermute | solution.py:165
  70.5 8.9 %all-gather.2 = f32[64,2048]{1,0:T(8,128)S(1)} all-gather(f32[16,2048]{1,0:T(8,128)S(1)} %fusion.50), channel_id=4, replica_groups=mesh['seq'=4,'exp'=8] {'seq'}, dimensions={0}, use_global_device_ids=true | all-gather | bytes 655360 | tf_op jit(solution)/shard_map/all_gather | solution.py:199
  79.7 15.1 %all_gather.39 = bf16[128,2048]{1,0:T(8,128)(2,1)S(1)} all-gather(bf16[16,2048]{1,0:T(8,128)(2,1)S(1)} %multiply_convert_fusion), channel_id=1, replica_groups=mesh['seq'=4,'exp'=8] {'exp'}, dimensions={0}, use_global_device_ids=true | all-gather | bytes 589824 | tf_op jit(solution)/shard_map/all_gather | solution.py:201
  95.2 6.1 %convolution_bitcast_fusion.2 = f32[8,128,352]{1,2,0:T(8,128)S(1)} fusion(bf16[8,2048,352]{1,2,0:T(8,128)(2,1)} %param.36, bf16[128,2048]{1,0:T(8,128)(2,1)S(1)} %all_gather.39), kind=kOutput, calls=%fused_computation.12 | convolution fusion | flops 1476395008 | bytes 13500416 | tf_op jit(solution)/shard_map/nd,jdf->jnf/dot_general | solution.py:218
  102.0 14.7 %convolution_bitcast_fusion = f32[128,2048]{1,0:T(8,128)S(1)} fusion(bf16[8,352,2048]{2,1,0:T(8,128)(2,1)} %param.38, bf16[8,2048,352]{1,2,0:T(8,128)(2,1)} %param.37, f32[8,128,352]{1,2,0:T(8,128)S(1)} %convolution_bitcast_fusion.2, f32[8,128]{1,0:T(8,128)S(1)} %select_reduce_fusion.4, bf16[128,2048]{1,0:T(8,128)(2,1)S(1)} %all_gather.39), kind=kOutput, calls=%fused_computation.8 | convolution fusion | flops 2955313152 | bytes 26087424 | tf_op jit(solution)/shard_map/jnf,jfd->nd/dot_general | solution.py:223
  116.7 2.9 %fusion.6 = f32[128,2048]{1,0:T(8,128)S(1)} fusion(f32[128,2048]{1,0:T(8,128)S(1)} %convolution_bitcast_fusion, s32[]{:T(128)S(6)} %select_n.111, bf16[352,2048]{1,0:T(8,128)(2,1)} %param.41, bf16[2048,352]{0,1:T(8,128)(2,1)} %param.40, bf16[128,2048]{1,0:T(8,128)(2,1)S(1)} %all_gather.39, f32[32,352]{1,0:T(8,128)S(1)} %fusion.37), kind=kOutput, calls=%fused_computation.10 | convolution fusion | flops 92407808 | bytes 3589120 | tf_op jit(solution)/shard_map/dot_general | solution.py:233
  121.4 3.5 %all-to-all-start.1 = ((bf16[32,4,2048]{2,1,0:T(4,128)(2,1)}), bf16[32,4,2048]{2,1,0:T(4,128)(2,1)S(1)}, u32[]{:S(2)}, u32[]{:S(2)}) async-start(bf16[32,4,2048]{2,1,0:T(4,128)(2,1)} %copy.162), calls=%async_computation.1 | async-start | bytes 1048576 | tf_op jit(solution)/shard_map/all_to_all | solution.py:242
  124.9 16.4 %all-to-all-done.1 = bf16[32,4,2048]{2,1,0:T(4,128)(2,1)S(1)} async-done(((bf16[32,4,2048]{2,1,0:T(4,128)(2,1)}), bf16[32,4,2048]{2,1,0:T(4,128)(2,1)S(1)}, u32[]{:S(2)}, u32[]{:S(2)}) %all-to-all-start.1) | async-done | bytes 524320 | tf_op jit(solution)/shard_map/all_to_all | solution.py:242
  141.7 14.0 %all-gather.5 = bf16[8,4,2048]{2,1,0:T(4,128)(2,1)S(1)} all-gather(bf16[1,4,2048]{2,1,0:T(4,128)(2,1)S(1)} %fusion.49), channel_id=5, replica_groups=mesh['seq'=4,'exp'=8] {'exp'}, dimensions={0}, use_global_device_ids=true | all-gather | bytes 147456 | tf_op jit(solution)/shard_map/all_gather | solution.py:44
  155.7 9.4 %all-gather.4 = bf16[32,4,2048]{2,1,0:T(4,128)(2,1)S(1)} all-gather(bf16[8,4,2048]{2,1,0:T(4,128)(2,1)S(1)} %all-gather.5), channel_id=6, replica_groups=mesh['seq'=4,'exp'=8] {'seq'}, dimensions={0}, use_global_device_ids=true | all-gather | bytes 655360 | tf_op jit(solution)/shard_map/all_gather | solution.py:45
  165.2 4.9 %convolution_reduce_fusion = f32[128]{0:T(128)S(1)} fusion(bf16[128,2048]{1,0:T(8,128)(2,1)S(1)} %reshape.582, bf16[2048,1600]{0,1:T(8,128)(2,1)} %param.43), kind=kOutput, calls=%fused_computation.16 | convolution fusion | flops 839065472 | bytes 7078400 | tf_op jit(solution)/shard_map/dot_general | solution.py:256
  170.1 9.3 %all_to_all.19 = f32[32,1,132]{2,1,0:T(1,128)S(1)} all-to-all(f32[32,1,132]{2,1,0:T(1,128)S(1)} %broadcast_in_dim.146), channel_id=1, replica_groups=mesh['seq'=4,'exp'=8] {'seq','exp'}, dimensions={0} | all-to-all | bytes 33792 | tf_op jit(solution)/shard_map/all_to_all | solution.py:258
  (130 shorter events, 18.6 us)
Async XLA Ops:
  0.6 69.5 %copy-start = (bf16[512,2048]{1,0:T(8,128)(2,1)S(1)}, bf16[512,2048]{1,0:T(8,128)(2,1)}, u32[]{:S(2)}) copy-start(bf16[512,2048]{1,0:T(8,128)(2,1)} %param.31) | copy-start | bytes 6291460
  7.6 7.9 %copy-start.10 = (s32[32]{0:T(128)S(1)}, s32[32]{0:T(128)}, u32[]{:S(2)}) copy-start(s32[32]{0:T(128)} %param.23) | copy-start | bytes 388
  9.1 21.7 %all-to-all-start = ((bf16[8,4,4,2048]{3,2,1,0:T(4,128)(2,1)}), bf16[8,4,4,2048]{3,2,1,0:T(4,128)(2,1)S(1)}, u32[]{:S(2)}, u32[]{:S(2)}) async-start(bf16[8,4,4,2048]{3,2,1,0:T(4,128)(2,1)} %select_select_fusion), calls=%async_computation | async-start | bytes 1048576 | tf_op jit(solution)/shard_map/all_to_all | solution.py:101
  24.3 4.2 %copy-start.6 = (s32[4,32,6]{1,0,2:T(4,128)S(1)}, s32[4,32,6]{1,0,2:T(4,128)}, u32[]{:S(2)}) copy-start(s32[4,32,6]{1,0,2:T(4,128)} %param.25) | copy-start | bytes 9220
  24.3 16.0 %copy-start.7 = (f32[2048]{0:T(1024)S(1)}, f32[2048]{0:T(1024)}, u32[]{:S(2)}) copy-start(f32[2048]{0:T(1024)} %param.27) | copy-start | bytes 24580
  40.5 2.4 %copy-start.3 = (bf16[512,2048]{1,0:T(8,128)(2,1)S(1)}, bf16[512,2048]{1,0:T(8,128)(2,1)}, u32[]{:S(2)}) copy-start(bf16[512,2048]{1,0:T(8,128)(2,1)} %copy.165) | copy-start | bytes 6291460
  40.5 3.2 %copy-start.2 = (bf16[512,2048]{1,0:T(8,128)(2,1)S(1)}, bf16[512,2048]{1,0:T(8,128)(2,1)}, u32[]{:S(2)}) copy-start(bf16[512,2048]{1,0:T(8,128)(2,1)} %copy.166) | copy-start | bytes 6291460
  61.1 4.1 %collective-permute-start = (f32[1,8320]{1,0:T(1,128)S(1)}, f32[1,8320]{1,0:T(1,128)S(1)}, u32[]{:S(2)}, u32[]{:S(2)}) collective-permute-start(f32[1,8320]{1,0:T(1,128)S(1)} %get-tuple-element.14), channel_id=1, source_target_pairs={{0,8},{8,0},{16,24},{24,16},{1,9},{9,1},{17,25},{25,17},{2,10},{10... | collective-permute-start | bytes 99848 | tf_op jit(solution)/shard_map/ppermute | solution.py:165
  61.5 3.9 %collective-permute-start.1 = (f32[1,8320]{1,0:T(1,128)S(1)}, f32[1,8320]{1,0:T(1,128)S(1)}, u32[]{:S(2)}, u32[]{:S(2)}) collective-permute-start(f32[1,8320]{1,0:T(1,128)S(1)} %get-tuple-element.13), channel_id=1, source_target_pairs={{0,16},{8,24},{16,0},{24,8},{1,17},{9,25},{17,1},{25,9},{2,18},{10... | collective-permute-start | bytes 99848 | tf_op jit(solution)/shard_map/ppermute | solution.py:165
  63.2 4.8 %collective-permute-start.2 = (f32[1,8320]{1,0:T(1,128)S(1)}, f32[1,8320]{1,0:T(1,128)S(1)}, u32[]{:S(2)}, u32[]{:S(2)}) collective-permute-start(f32[1,8320]{1,0:T(1,128)S(1)} %get-tuple-element.12), channel_id=1, source_target_pairs={{0,24},{8,16},{16,8},{24,0},{1,25},{9,17},{17,9},{25,1},{2,26},{10... | collective-permute-start | bytes 99848 | tf_op jit(solution)/shard_map/ppermute | solution.py:165
  70.1 9.6 %copy-start.8 = (f32[2048]{0:T(1024)S(1)}, f32[2048]{0:T(1024)}, u32[]{:S(2)}) copy-start(f32[2048]{0:T(1024)} %param.34) | copy-start | bytes 24580
  70.1 24.8 %copy-start.5 = (bf16[2048,64]{0,1:T(8,128)(2,1)S(1)}, bf16[2048,64]{0,1:T(8,128)(2,1)}, u32[]{:S(2)}) copy-start(bf16[2048,64]{0,1:T(8,128)(2,1)} %param.35) | copy-start | bytes 786436
  95.2 6.3 %copy-start.4 = (bf16[2048,352]{0,1:T(8,128)(2,1)S(1)}, bf16[2048,352]{0,1:T(8,128)(2,1)}, u32[]{:S(2)}) copy-start(bf16[2048,352]{0,1:T(8,128)(2,1)} %param.39) | copy-start | bytes 4325380
  119.9 21.7 %copy-start.9 = (f32[2048]{0:T(1024)S(1)}, f32[2048]{0:T(1024)}, u32[]{:S(2)}) copy-start(f32[2048]{0:T(1024)} %param.42) | copy-start | bytes 24580
  121.4 19.8 %all-to-all-start.1 = ((bf16[32,4,2048]{2,1,0:T(4,128)(2,1)}), bf16[32,4,2048]{2,1,0:T(4,128)(2,1)S(1)}, u32[]{:S(2)}, u32[]{:S(2)}) async-start(bf16[32,4,2048]{2,1,0:T(4,128)(2,1)} %copy.162), calls=%async_computation.1 | async-start | bytes 1048576 | tf_op jit(solution)/shard_map/all_to_all | solution.py:242
  165.2 15.6 %copy-start.1 = (bf16[512,2048]{1,0:T(8,128)(2,1)S(1)}, bf16[512,2048]{1,0:T(8,128)(2,1)}, u32[]{:S(2)}) copy-start(bf16[512,2048]{1,0:T(8,128)(2,1)} %param.31) | copy-start | bytes 6291460
